TPU v7x, 128 devices: a whole 4x4x4 slice. The times are simulated.
128 devices in a mesh: expert: 32 (over y, z, core), dp: 4 (over x).
Axes of the slice: x: 4, y: 4, z: 4, core: 2. Of those that a mesh axis runs over, the one named last changes fastest.
Arguments:
- activations: bfloat16 [2048, 7168], P(('expert', 'dp')), may hold values from -6 to 6
- cotangent: bfloat16 [2048, 7168], P(('expert', 'dp')), may hold values from -6 to 6
- route_ids: int32 [2048, 8], P(('expert', 'dp')), may hold values from 0 to 31, all different within a row; in each aligned block of 16 rows (0 to 15, 16 to 31, ...) at most 5 rows name the same one
- route_weights: float32 [2048, 8], P(('expert', 'dp')), may hold values from 0.05 to 0.6
- gate_weights: bfloat16 [32, 7168, 1024], P('expert', 'dp'), may hold values from -0.0625 to 0.0625
- up_weights: bfloat16 [32, 7168, 1024], P('expert', 'dp'), may hold values from -0.0625 to 0.0625
- down_weights: bfloat16 [32, 1024, 7168], P('expert', None, 'dp'), may hold values from -0.1875 to 0.1875
Outputs:
- grad_input: bfloat16 [2048, 7168], P(('expert', 'dp'))
- grad_gate: bfloat16 [32, 7168, 1024], P('expert', 'dp')
- grad_up: bfloat16 [32, 7168, 1024], P('expert', 'dp')
- grad_down: bfloat16 [32, 1024, 7168], P('expert', None, 'dp')
Inputs may be any that keep to these rules, and one draw needn't show every extreme that they name: `route_ids`: each token names 8 different experts. Among the routes of one device's 16 tokens, no expert is named more than 5 times, a bound that some block reaches.
All inputs are finite; a program needn't handle non-finite values.
Results may differ from a plain program's by a relative error of at most 0.0064.
Values may be sent and summed in bfloat16 or wider, within the bound.
No kernel may reach another device: no remote copies, remote signals or barrier semaphores. Data moves between devices by JAX's collectives and lax.ppermute only.
A program may use at most 128 MiB of HBM per device.

v0:
```python
import jax
import jax.numpy as jnp
from jax import lax
from jax.sharding import PartitionSpec as P


def swiglu_back(gate, upper, upstream):
    sigma = jax.nn.sigmoid(gate)
    silu_gate = gate * sigma
    activated = (silu_gate * upper).astype(jnp.bfloat16)
    grad_pre = (upstream * upper * sigma * (1.0 + gate * (1.0 - sigma))).astype(jnp.bfloat16)
    grad_lin = (upstream * silu_gate).astype(jnp.bfloat16)
    return (grad_pre, grad_lin, activated)


def contract_rows(left, right):
    return lax.dot_general(
        left, right, (((0,), (0,)), ((), ())), preferred_element_type=jnp.float32
    )


def shards(
    activations, cotangent, route_ids, route_weights, gate_weights, up_weights, down_weights
):
    tok_rows, width = activations.shape
    topk = route_ids.shape[1]
    num_dp = lax.axis_size("dp")
    num_exp = lax.axis_size("expert")
    slice_width = gate_weights.shape[1]
    hidden = gate_weights.shape[2]
    capacity = min(tok_rows, 5 * tok_rows * topk // (4 * num_exp))
    buffer_rows = num_exp * num_dp * capacity
    flat_ids = route_ids.reshape(-1)
    expert_iota = jnp.arange(num_exp, dtype=jnp.int32)
    onehot = (flat_ids[:, None] == expert_iota[None, :]).astype(jnp.int32)
    before = jnp.cumsum(onehot, axis=0) - onehot
    slot = jnp.sum(before * onehot, axis=1)
    target = (flat_ids * capacity + slot).reshape(tok_rows, topk)
    slot_iota = jnp.arange(num_exp * capacity, dtype=jnp.int32)
    matches = target[:, :, None] == slot_iota[None, None, :]
    placing = jnp.any(matches, axis=1).astype(jnp.bfloat16)
    slot_weight = jnp.sum(jnp.where(matches, route_weights[:, :, None], 0.0), axis=(0, 1))
    send_act = contract_rows(placing, activations).astype(jnp.bfloat16)
    send_cot = (contract_rows(placing, cotangent) * slot_weight[:, None]).astype(jnp.bfloat16)
    send_act = send_act.reshape(num_exp, capacity, num_dp, slice_width)
    send_cot = send_cot.reshape(num_exp, capacity, num_dp, slice_width)
    flat_act = jnp.swapaxes(send_act, 1, 2).reshape(num_exp * num_dp, capacity, slice_width)
    flat_cot = jnp.swapaxes(send_cot, 1, 2).reshape(num_exp * num_dp, capacity, slice_width)
    recv_act, recv_cot = (
        lax.all_to_all(flat_act, ("expert", "dp"), split_axis=0, concat_axis=0, tiled=True),
        lax.all_to_all(flat_cot, ("expert", "dp"), split_axis=0, concat_axis=0, tiled=True),
    )
    recv_act = recv_act.reshape(buffer_rows, slice_width)
    recv_cot = recv_cot.reshape(buffer_rows, slice_width)
    gate_local = gate_weights[0]
    up_local = up_weights[0]
    down_local = down_weights[0]
    act_rows = recv_act
    cot_rows = recv_cot
    gate_part = jnp.dot(act_rows, gate_local, preferred_element_type=jnp.float32)
    up_part = jnp.dot(act_rows, up_local, preferred_element_type=jnp.float32)
    back_part = lax.dot_general(
        cot_rows, down_local, (((1,), (1,)), ((), ())), preferred_element_type=jnp.float32
    )
    summed = lax.psum(jnp.concatenate([gate_part, up_part, back_part], axis=1), "dp")
    grad_pre, grad_lin, activated = swiglu_back(
        summed[:, :hidden], summed[:, hidden : 2 * hidden], summed[:, 2 * hidden :]
    )
    act_rows = recv_act
    cot_rows = recv_cot
    rows_back = lax.dot_general(
        grad_pre, gate_local, (((1,), (1,)), ((), ())), preferred_element_type=jnp.float32
    ) + lax.dot_general(
        grad_lin, up_local, (((1,), (1,)), ((), ())), preferred_element_type=jnp.float32
    )
    grad_gate = contract_rows(act_rows, grad_pre).astype(jnp.bfloat16)[None]
    grad_up = contract_rows(act_rows, grad_lin).astype(jnp.bfloat16)[None]
    grad_down = contract_rows(activated, cot_rows).astype(jnp.bfloat16)[None]
    back_rows = rows_back.astype(jnp.bfloat16)
    flat_back = back_rows.reshape(num_exp * num_dp, capacity, slice_width)
    arrived = lax.all_to_all(flat_back, ("expert", "dp"), split_axis=0, concat_axis=0, tiled=True)
    arrived = jnp.swapaxes(arrived.reshape(num_exp, num_dp, capacity, slice_width), 1, 2)
    arrived = arrived.reshape(num_exp * capacity, width)
    grad_input = jnp.dot(placing, arrived, preferred_element_type=jnp.float32).astype(jnp.bfloat16)
    return (grad_input, grad_gate, grad_up, grad_down)


def solution(mesh):
    placed = (
        P(("expert", "dp"), None),
        P(("expert", "dp"), None),
        P(("expert", "dp"), None),
        P(("expert", "dp"), None),
        P("expert", "dp", None),
        P("expert", "dp", None),
        P("expert", None, "dp"),
    )
    return jax.shard_map(
        shards,
        mesh=mesh,
        in_specs=placed,
        out_specs=(
            P(("expert", "dp"), None),
            P("expert", "dp", None),
            P("expert", "dp", None),
            P("expert", None, "dp"),
        ),
        check_vma=False,
    )
```

profile of v0, /device:TPU:1, one launch (start us, length us, event | category | flops | bytes accessed | tf_op | source)
XLA Modules:
  0.0 371.8 jit_solution(10881495854793656829)
XLA Ops:
  7.2 0.0 copy-start
  7.2 0.8 copy.30
  8.0 0.1 eq.28
  8.1 0.1 fusion.19
  8.2 0.2 reduce_window_sum.11
  8.3 0.2 select_reduce_fusion.1
  8.5 0.1 reduce_sum.21
  8.6 0.1 fusion.18
  8.8 2.2 convolution_convert_fusion
  10.9 3.5 reshape.45
  14.4 2.5 copy.38
  16.9 11.9 %all-to-all-start = ((bf16[128,5,1792]{2,1,0:T(8,128)(2,1)}), bf16[128,5,1792]{2,1,0:T(8,128)(2,1)}, u32[]{:S(2)}, u32[]{:S(2)}) async-start(bf16[128,5,1792]{2,1,0:T(8,128)(2,1)} %bitcast.49), calls=%async_computation | async-start | bytes 7340032 | tf_op jit(solution)/shard_map/all_to_all | solution.py:50
  28.8 0.1 copy.34
  28.9 0.1 select_reduce_fusion
  29.0 0.8 fusion
  29.8 2.9 reshape.48
  32.8 4.2 %copy.39 = bf16[32,4,5,1792]{3,2,1,0:T(8,128)(2,1)} copy(bf16[32,4,5,1792]{3,1,2,0:T(4,128)(2,1)} %bitcast.52) | data formatting | bytes 4587520 | tf_op jit(solution)/shard_map/reshape | solution.py:48
  36.9 39.4 %all-to-all-done = bf16[128,5,1792]{2,1,0:T(8,128)(2,1)} async-done(((bf16[128,5,1792]{2,1,0:T(8,128)(2,1)}), bf16[128,5,1792]{2,1,0:T(8,128)(2,1)}, u32[]{:S(2)}, u32[]{:S(2)}) %all-to-all-start) | async-done | bytes 2293792 | tf_op jit(solution)/shard_map/all_to_all | solution.py:50
  76.4 4.7 %all-to-all-start.1 = ((bf16[128,5,1792]{2,1,0:T(8,128)(2,1)}), bf16[128,5,1792]{2,1,0:T(8,128)(2,1)}, u32[]{:S(2)}, u32[]{:S(2)}) async-start(bf16[128,5,1792]{2,1,0:T(8,128)(2,1)} %bitcast.48), calls=%async_computation.1 | async-start | bytes 7340032 | tf_op jit(solution)/shard_map/all_to_all | solution.py:51
  81.1 0.2 all-reduce.2.cloned.1.call-start
  81.3 5.4 %reshape.47 = bf16[640,1792]{1,0:T(8,128)(2,1)} reshape(bf16[128,5,1792]{2,1,0:T(8,128)(2,1)} %all-to-all-done) | data formatting | bytes 4587520 | tf_op jit(solution)/shard_map/reshape | solution.py:53
  86.7 5.4 %fusion.5 = f32[640,1024]{1,0:T(8,128)S(1)} fusion(bf16[640,1792]{1,0:T(8,128)(2,1)} %reshape.47, bf16[1,1792,1024]{2,1,0:T(8,128)(2,1)} %param.12), kind=kOutput, calls=%fused_computation.13 | convolution fusion | flops 2348810240 | bytes 8585216 | tf_op jit(solution)/shard_map/dot_general | solution.py:61
  92.1 4.0 %fusion.9 = f32[640,1024]{1,0:T(8,128)} fusion(bf16[640,1792]{1,0:T(8,128)(2,1)S(1)} %copy-done.3, bf16[1,1792,1024]{2,1,0:T(8,128)(2,1)S(1)} %copy-done.12), kind=kOutput, calls=%fused_computation.17 | convolution fusion | flops 2348810240 | bytes 8585216 | tf_op jit(solution)/shard_map/dot_general | solution.py:60
  96.1 32.5 %all-to-all-done.1 = bf16[128,5,1792]{2,1,0:T(8,128)(2,1)} async-done(((bf16[128,5,1792]{2,1,0:T(8,128)(2,1)}), bf16[128,5,1792]{2,1,0:T(8,128)(2,1)}, u32[]{:S(2)}, u32[]{:S(2)}) %all-to-all-start.1) | async-done | bytes 2293792 | tf_op jit(solution)/shard_map/all_to_all | solution.py:51
  128.6 5.4 %reshape.50 = bf16[640,1792]{1,0:T(8,128)(2,1)} reshape(bf16[128,5,1792]{2,1,0:T(8,128)(2,1)} %all-to-all-done.1) | data formatting | bytes 4587520 | tf_op jit(solution)/shard_map/reshape | solution.py:54
  134.0 5.4 %fusion.1 = f32[640,1024]{1,0:T(8,128)S(1)} fusion(bf16[640,1792]{1,0:T(8,128)(2,1)} %reshape.50, bf16[1,1024,1792]{2,1,0:T(8,128)(2,1)} %param.13), kind=kOutput, calls=%fused_computation.9 | convolution fusion | flops 2348810240 | bytes 8585216 | tf_op jit(solution)/shard_map/dot_general | solution.py:62
  139.5 3.5 pad_maximum_fusion
  142.9 0.0 all-reduce.2.cloned.1.call-update
  142.9 147.8 %all-reduce.2.cloned.1.call-done = f32[640,3072]{1,0:T(8,128)} async-done(((f32[640,3072]{1,0:T(8,128)}), f32[640,3072]{1,0:T(8,128)}) %all-reduce.2.cloned.1.call-update) | async-done | bytes 7864336 | tf_op jit(solution)/shard_map/psum | solution.py:65
  290.7 5.0 %multiply_convert_fusion.2 = (bf16[640,1024]{1,0:T(8,128)(2,1)S(1)}, bf16[640,1024]{1,0:T(8,128)(2,1)S(1)}) fusion(f32[640,3072]{1,0:T(8,128)} %all-reduce.2.cloned.1.call-done), kind=kLoop, calls=%fused_computation.24 | loop fusion | flops 8519680 | bytes 10485760 | tf_op jit(solution)/shard_map/convert_element_type | solution.py:11
  295.7 0.0 copy-start.8
  295.8 0.0 copy-done.11
  295.8 0.0 copy-start.13
  295.8 2.6 fusion.3
  298.4 0.3 copy-done.13
  298.7 2.6 add_convert_fusion
  301.3 2.7 reshape.51
  304.1 8.9 %all-to-all-start.2 = ((bf16[128,5,1792]{2,1,0:T(8,128)(2,1)}), bf16[128,5,1792]{2,1,0:T(8,128)(2,1)}, u32[]{:S(2)}, u32[]{:S(2)}) async-start(bf16[128,5,1792]{2,1,0:T(8,128)(2,1)} %reshape.51), calls=%async_computation.2 | async-start | bytes 7340032 | tf_op jit(solution)/shard_map/all_to_all | solution.py:81
  313.0 5.9 %fusion.11 = bf16[1,1792,1024]{2,1,0:T(8,128)(2,1)} fusion(bf16[640,1792]{1,0:T(8,128)(2,1)S(1)} %copy-done.4, bf16[640,1024]{1,0:T(8,128)(2,1)} %copy-done.8), kind=kOutput, calls=%fused_computation.19 | convolution fusion | flops 2350645248 | bytes 7274496 | tf_op jit(solution)/shard_map/dot_general | solution.py:17
  318.9 0.0 copy-done.7
  318.9 4.5 %fusion.12 = bf16[1,1792,1024]{2,1,0:T(8,128)(2,1)} fusion(bf16[640,1792]{1,0:T(8,128)(2,1)S(1)} %copy-done.4, bf16[640,1024]{1,0:T(8,128)(2,1)S(1)} %copy-done.7), kind=kOutput, calls=%fused_computation.20 | convolution fusion | flops 2350645248 | bytes 7274496 | tf_op jit(solution)/shard_map/dot_general | solution.py:17
  323.5 0.0 copy-done.5
  323.5 7.6 %fusion.13 = bf16[1,1024,1792]{2,1,0:T(8,128)(2,1)} fusion(bf16[640,1792]{1,0:T(8,128)(2,1)S(1)} %copy-done.5, f32[640,3072]{1,0:T(8,128)} %all-reduce.2.cloned.1.call-done), kind=kOutput, calls=%fused_computation.21 | convolution fusion | flops 2354577408 | bytes 11206656 | tf_op jit(solution)/shard_map/dot_general | solution.py:17
  331.1 29.4 %all-to-all-done.2 = bf16[128,5,1792]{2,1,0:T(8,128)(2,1)} async-done(((bf16[128,5,1792]{2,1,0:T(8,128)(2,1)}), bf16[128,5,1792]{2,1,0:T(8,128)(2,1)}, u32[]{:S(2)}, u32[]{:S(2)}) %all-to-all-start.2) | async-done | bytes 2293792 | tf_op jit(solution)/shard_map/all_to_all | solution.py:81
  360.5 3.0 copy.37
  363.5 0.0 copy-start.1
  363.5 0.3 copy.42
  363.8 1.1 convolution_convert_fusion.1
  (21 shorter events, 0.1 us)
Async XLA Ops:
  7.2 1.6 copy-start
  16.9 11.9 %copy-start.10 = (f32[16,8]{0,1:T(8,128)S(1)}, f32[16,8]{0,1:T(8,128)}, u32[]{:S(2)}) copy-start(f32[16,8]{0,1:T(8,128)} %param.10) | copy-start | bytes 1540
  16.9 12.1 %copy-start.9 = (bf16[16,7168]{1,0:T(8,128)(2,1)S(1)}, bf16[16,7168]{1,0:T(8,128)(2,1)}, u32[]{:S(2)}) copy-start(bf16[16,7168]{1,0:T(8,128)(2,1)} %param.8) | copy-start | bytes 688132
  16.9 59.4 %all-to-all-start = ((bf16[128,5,1792]{2,1,0:T(8,128)(2,1)}), bf16[128,5,1792]{2,1,0:T(8,128)(2,1)}, u32[]{:S(2)}, u32[]{:S(2)}) async-start(bf16[128,5,1792]{2,1,0:T(8,128)(2,1)} %bitcast.49), calls=%async_computation | async-start | bytes 7340032 | tf_op jit(solution)/shard_map/all_to_all | solution.py:50
  76.4 52.3 %all-to-all-start.1 = ((bf16[128,5,1792]{2,1,0:T(8,128)(2,1)}), bf16[128,5,1792]{2,1,0:T(8,128)(2,1)}, u32[]{:S(2)}, u32[]{:S(2)}) async-start(bf16[128,5,1792]{2,1,0:T(8,128)(2,1)} %bitcast.48), calls=%async_computation.1 | async-start | bytes 7340032 | tf_op jit(solution)/shard_map/all_to_all | solution.py:51
  81.1 209.7 %all-reduce.2.cloned.1.call-start = ((), (), s32[]{:S(2)}) async-start(), calls=%async_computation.3 | async-start | bytes 15728640 | tf_op jit(solution)/shard_map/psum | solution.py:65
  86.7 5.4 %copy-start.3 = (bf16[640,1792]{1,0:T(8,128)(2,1)S(1)}, bf16[640,1792]{1,0:T(8,128)(2,1)}, u32[]{:S(2)}) copy-start(bf16[640,1792]{1,0:T(8,128)(2,1)} %reshape.47) | copy-start | bytes 6881284
  86.7 5.4 %copy-start.12 = (bf16[1,1792,1024]{2,1,0:T(8,128)(2,1)S(1)}, bf16[1,1792,1024]{2,1,0:T(8,128)(2,1)}, u32[]{:S(2)}) copy-start(bf16[1,1792,1024]{2,1,0:T(8,128)(2,1)} %param.11) | copy-start | bytes 11010052
  134.0 5.4 %copy-start.2 = (f32[640,1024]{1,0:T(8,128)S(1)}, f32[640,1024]{1,0:T(8,128)}, u32[]{:S(2)}) copy-start(f32[640,1024]{1,0:T(8,128)} %fusion.9) | copy-start | bytes 7864324
  290.7 5.1 %copy-start.11 = (bf16[1,1792,1024]{2,1,0:T(8,128)(2,1)S(1)}, bf16[1,1792,1024]{2,1,0:T(8,128)(2,1)}, u32[]{:S(2)}) copy-start(bf16[1,1792,1024]{2,1,0:T(8,128)(2,1)} %param.12) | copy-start | bytes 11010052
  295.7 2.6 copy-start.6
  295.7 2.6 copy-start.8
  295.8 3.0 copy-start.13
  304.1 8.9 %copy-start.4 = (bf16[640,1792]{1,0:T(8,128)(2,1)S(1)}, bf16[640,1792]{1,0:T(8,128)(2,1)}, u32[]{:S(2)}) copy-start(bf16[640,1792]{1,0:T(8,128)(2,1)} %reshape.47) | copy-start | bytes 6881284
  304.1 56.4 %all-to-all-start.2 = ((bf16[128,5,1792]{2,1,0:T(8,128)(2,1)}), bf16[128,5,1792]{2,1,0:T(8,128)(2,1)}, u32[]{:S(2)}, u32[]{:S(2)}) async-start(bf16[128,5,1792]{2,1,0:T(8,128)(2,1)} %reshape.51), calls=%async_computation.2 | async-start | bytes 7340032 | tf_op jit(solution)/shard_map/all_to_all | solution.py:81
  313.0 6.0 %copy-start.7 = (bf16[640,1024]{1,0:T(8,128)(2,1)S(1)}, bf16[640,1024]{1,0:T(8,128)(2,1)}, u32[]{:S(2)}) copy-start(bf16[640,1024]{1,0:T(8,128)(2,1)} %copy-done.6) | copy-start | bytes 3932164
  318.9 4.5 %copy-start.5 = (bf16[640,1792]{1,0:T(8,128)(2,1)S(1)}, bf16[640,1792]{1,0:T(8,128)(2,1)}, u32[]{:S(2)}) copy-start(bf16[640,1792]{1,0:T(8,128)(2,1)} %reshape.50) | copy-start | bytes 6881284
  363.5 1.4 copy-start.1
Sparse Core Ops, SparseCore 0:
  143.1 147.5 all-reduce.1
where the time goes:
time: 373 us; the launch traced here: 372 us
  waiting for transfers between devices  249 us (67%)
  matrix products  42.2 us (11%)
  local copies, waits for them, and re-layouts  31.3 us (8%)
  starting transfers between devices  25.7 us (7%)
  between operations  14.3 us (4%)
  other arithmetic  9.16 us (2%)
    psum x1, waiting for transfers between devices, shards(): lax.psum(jnp.concatenate([gate_part, up_part, back_part], axis=1), 'dp')  148 us
    all_to_all x1, waiting for transfers between devices, shards(): lax.all_to_all(flat_act, ('expert', 'dp'), split_axis=0, concat_axis=0, t...  39.4 us
    all_to_all x1, waiting for transfers between devices, shards(): lax.all_to_all(flat_cot, ('expert', 'dp'), split_axis=0, concat_axis=0, t...  32.5 us
    all_to_all x1, waiting for transfers between devices, shards(): lax.all_to_all(flat_back, ('expert', 'dp'), split_axis=0, concat_axis=0,...  29.4 us
    dot_general x5, matrix products, contract_rows(): lax.dot_general(left, right, (((0,), (0,)), ((), ())), preferred_element_...  21.1 us
    all_to_all x1, starting transfers between devices, shards(): lax.all_to_all(flat_act, ('expert', 'dp'), split_axis=0, concat_axis=0, t...  11.9 us
    all_to_all x1, starting transfers between devices, shards(): lax.all_to_all(flat_back, ('expert', 'dp'), split_axis=0, concat_axis=0,...  8.88 us
  transfers between devices with their start and end apart: 4, of which 4 were waited for; matrix products, arithmetic and copies ran while one was open for 11% of the time, Pallas kernels for 0%

commit v1 on v0

--- a/solution.py
+++ b/solution.py
@@ -1,7 +1,16 @@
+import functools
 import jax
 import jax.numpy as jnp
 from jax import lax
 from jax.sharding import PartitionSpec as P
+
+
+def perform_the_keys(my_tile, dev_axis):
+    v1 = jax.lax.all_gather(my_tile, dev_axis)
+    return jnp.sum(v1, axis=0)
+
+
+produce_sample_on_mesh = functools.partial(perform_the_keys, dev_axis="dp")
 
 
 def swiglu_back(gate, upper, upstream):
@@ -62,7 +71,7 @@
     back_part = lax.dot_general(
         cot_rows, down_local, (((1,), (1,)), ((), ())), preferred_element_type=jnp.float32
     )
-    summed = lax.psum(jnp.concatenate([gate_part, up_part, back_part], axis=1), "dp")
+    summed = produce_sample_on_mesh(jnp.concatenate([gate_part, up_part, back_part], axis=1))
     grad_pre, grad_lin, activated = swiglu_back(
         summed[:, :hidden], summed[:, hidden : 2 * hidden], summed[:, 2 * hidden :]
     )

time: 373 us -> 513 us (1.38)
  waiting for transfers between devices: 249 us -> 373 us
  other arithmetic: 9.16 us -> 24.3 us
    all_gather x0 -> x1, waiting for transfers between devices: none -> 271 us  [perform_the_keys(): v1 = jax.lax.all_gather(my_tile, dev_axis)]
    psum x1 -> x0, waiting for transfers between devices: 148 us -> none  [shards(): lax.psum(jnp.concatenate([gate_part, up_part, back_part], axis=1), 'dp')]
    reduce_sum x0 -> x1, other arithmetic: none -> 15.1 us  [perform_the_keys(): return jnp.sum(v1, axis=0)]
  transfers between devices with their start and end apart: 4 -> 4, of which waited for: 4 -> 4; matrix products, arithmetic and copies ran while one was open for 11% -> 8% of each run, Pallas kernels for 0% -> 0%
where the time goes in v1:
time: 513 us; the launch traced here: 512 us
  waiting for transfers between devices  373 us (73%)
  matrix products  42.3 us (8%)
  local copies, waits for them, and re-layouts  31.5 us (6%)
  starting transfers between devices  26.6 us (5%)
  other arithmetic  24.3 us (5%)
  between operations  14.3 us (3%)
    all_gather x1, waiting for transfers between devices, perform_the_keys(): v1 = jax.lax.all_gather(my_tile, dev_axis)  271 us
    all_to_all x1, waiting for transfers between devices, shards(): lax.all_to_all(flat_act, ('expert', 'dp'), split_axis=0, concat_axis=0, t...  39.4 us
    all_to_all x1, waiting for transfers between devices, shards(): lax.all_to_all(flat_cot, ('expert', 'dp'), split_axis=0, concat_axis=0, t...  32.5 us
    all_to_all x1, waiting for transfers between devices, shards(): lax.all_to_all(flat_back, ('expert', 'dp'), split_axis=0, concat_axis=0,...  29.4 us
    dot_general x5, matrix products, contract_rows(): lax.dot_general(left, right, (((0,), (0,)), ((), ())), preferred_element_...  21.1 us
    reduce_sum x1, other arithmetic, perform_the_keys(): return jnp.sum(v1, axis=0)  15.1 us
    all_to_all x1, starting transfers between devices, shards(): lax.all_to_all(flat_act, ('expert', 'dp'), split_axis=0, concat_axis=0, t...  11.9 us
  transfers between devices with their start and end apart: 4, of which 4 were waited for; matrix products, arithmetic and copies ran while one was open for 8% of the time, Pallas kernels for 0%

profile of v1, /device:TPU:1, one launch (start us, length us, event | category | flops | bytes accessed | tf_op | source)
XLA Modules:
  0.0 511.7 jit_solution(5905297552611053820)
XLA Ops:
  7.2 0.0 copy-start
  7.2 0.8 copy.30
  8.0 0.1 eq.28
  8.1 0.1 fusion.19
  8.2 0.2 reduce_window_sum.11
  8.3 0.2 select_reduce_fusion.1
  8.5 0.1 reduce_sum.30
  8.6 0.1 fusion.18
  8.8 2.2 convolution_convert_fusion
  10.9 3.5 reshape.45
  14.4 2.5 copy.38
  16.9 11.9 %all-to-all-start = ((bf16[128,5,1792]{2,1,0:T(8,128)(2,1)}), bf16[128,5,1792]{2,1,0:T(8,128)(2,1)}, u32[]{:S(2)}, u32[]{:S(2)}) async-start(bf16[128,5,1792]{2,1,0:T(8,128)(2,1)} %bitcast.51), calls=%async_computation | async-start | bytes 7340032 | tf_op jit(solution)/shard_map/all_to_all | solution.py:59
  28.8 0.1 copy.34
  28.9 0.1 select_reduce_fusion
  29.0 0.8 fusion
  29.8 2.9 reshape.48
  32.8 4.2 copy.39
  36.9 39.4 %all-to-all-done = bf16[128,5,1792]{2,1,0:T(8,128)(2,1)} async-done(((bf16[128,5,1792]{2,1,0:T(8,128)(2,1)}), bf16[128,5,1792]{2,1,0:T(8,128)(2,1)}, u32[]{:S(2)}, u32[]{:S(2)}) %all-to-all-start) | async-done | bytes 2293792 | tf_op jit(solution)/shard_map/all_to_all | solution.py:59
  76.4 4.7 all-to-all-start.1
  81.1 0.2 all-gather.3.cloned.1.call-start
  81.3 5.4 %reshape.47 = bf16[640,1792]{1,0:T(8,128)(2,1)} reshape(bf16[128,5,1792]{2,1,0:T(8,128)(2,1)} %all-to-all-done) | data formatting | bytes 4587520 | tf_op jit(solution)/shard_map/reshape | solution.py:62
  86.7 5.4 %fusion.5 = f32[640,1024]{1,0:T(8,128)S(1)} fusion(bf16[640,1792]{1,0:T(8,128)(2,1)} %reshape.47, bf16[1,1792,1024]{2,1,0:T(8,128)(2,1)} %param.12), kind=kOutput, calls=%fused_computation.13 | convolution fusion | flops 2348810240 | bytes 8585216 | tf_op jit(solution)/shard_map/dot_general | solution.py:70
  92.1 4.0 fusion.9
  96.1 32.5 %all-to-all-done.1 = bf16[128,5,1792]{2,1,0:T(8,128)(2,1)} async-done(((bf16[128,5,1792]{2,1,0:T(8,128)(2,1)}), bf16[128,5,1792]{2,1,0:T(8,128)(2,1)}, u32[]{:S(2)}, u32[]{:S(2)}) %all-to-all-start.1) | async-done | bytes 2293792 | tf_op jit(solution)/shard_map/all_to_all | solution.py:60
  128.6 5.4 %reshape.50 = bf16[640,1792]{1,0:T(8,128)(2,1)} reshape(bf16[128,5,1792]{2,1,0:T(8,128)(2,1)} %all-to-all-done.1) | data formatting | bytes 4587520 | tf_op jit(solution)/shard_map/reshape | solution.py:63
  134.0 5.4 %fusion.1 = f32[640,1024]{1,0:T(8,128)S(1)} fusion(bf16[640,1792]{1,0:T(8,128)(2,1)} %reshape.50, bf16[1,1024,1792]{2,1,0:T(8,128)(2,1)} %param.13), kind=kOutput, calls=%fused_computation.9 | convolution fusion | flops 2348810240 | bytes 8585216 | tf_op jit(solution)/shard_map/dot_general | solution.py:71
  139.5 3.4 pad_maximum_fusion
  142.9 0.0 all-gather.3.cloned.1.call-update
  142.9 271.5 %all-gather.3.cloned.1.call-done = f32[2560,3072]{1,0:T(8,128)} async-done(((f32[640,3072]{1,0:T(8,128)}), f32[2560,3072]{1,0:T(8,128)}) %all-gather.3.cloned.1.call-update) | async-done | bytes 31457296 | tf_op jit(solution)/shard_map/all_gather | solution.py:9
  414.4 15.1 %reduce_sum.32 = f32[640,3072]{1,0:T(8,128)} reduce(f32[4,640,3072]{2,1,0:T(8,128)} %bitcast.49, f32[]{:T(128)} %constant.12.clone.1), dimensions={0}, to_apply=%region_4.5 | reduce | flops 5898240 | bytes 39321604 | tf_op jit(solution)/shard_map/reduce_sum | solution.py:10
  429.5 5.0 multiply_convert_fusion.2
  434.6 0.0 copy-start.8
  434.6 0.0 copy-done.11
  434.6 0.0 copy-start.13
  434.6 2.6 fusion.3
  437.2 0.3 copy-done.13
  437.6 2.6 add_convert_fusion
  440.2 2.9 reshape.51
  443.1 9.8 %all-to-all-start.2 = ((bf16[128,5,1792]{2,1,0:T(8,128)(2,1)}), bf16[128,5,1792]{2,1,0:T(8,128)(2,1)}, u32[]{:S(2)}, u32[]{:S(2)}) async-start(bf16[128,5,1792]{2,1,0:T(8,128)(2,1)} %reshape.51), calls=%async_computation.2 | async-start | bytes 7340032 | tf_op jit(solution)/shard_map/all_to_all | solution.py:90
  452.9 0.0 copy-done.4
  453.0 5.9 %fusion.11 = bf16[1,1792,1024]{2,1,0:T(8,128)(2,1)} fusion(bf16[640,1792]{1,0:T(8,128)(2,1)S(1)} %copy-done.4, bf16[640,1024]{1,0:T(8,128)(2,1)} %copy-done.8), kind=kOutput, calls=%fused_computation.19 | convolution fusion | flops 2350645248 | bytes 7274496 | tf_op jit(solution)/shard_map/dot_general | solution.py:26
  458.9 4.5 fusion.12
  463.4 7.7 %fusion.13 = bf16[1,1024,1792]{2,1,0:T(8,128)(2,1)} fusion(bf16[640,1792]{1,0:T(8,128)(2,1)S(1)} %copy-done.5, f32[640,3072]{1,0:T(8,128)} %reduce_sum.32), kind=kOutput, calls=%fused_computation.21 | convolution fusion | flops 2354577408 | bytes 11206656 | tf_op jit(solution)/shard_map/dot_general | solution.py:26
  471.1 29.4 %all-to-all-done.2 = bf16[128,5,1792]{2,1,0:T(8,128)(2,1)} async-done(((bf16[128,5,1792]{2,1,0:T(8,128)(2,1)}), bf16[128,5,1792]{2,1,0:T(8,128)(2,1)}, u32[]{:S(2)}, u32[]{:S(2)}) %all-to-all-start.2) | async-done | bytes 2293792 | tf_op jit(solution)/shard_map/all_to_all | solution.py:90
  500.5 3.0 copy.37
  503.4 0.0 copy-start.1
  503.4 0.3 copy.42
  503.8 1.1 convolution_convert_fusion.1
  (22 shorter events, 0.1 us)
Async XLA Ops:
  7.2 1.6 copy-start
  16.9 11.9 %copy-start.10 = (f32[16,8]{0,1:T(8,128)S(1)}, f32[16,8]{0,1:T(8,128)}, u32[]{:S(2)}) copy-start(f32[16,8]{0,1:T(8,128)} %param.10) | copy-start | bytes 1540
  16.9 12.1 %copy-start.9 = (bf16[16,7168]{1,0:T(8,128)(2,1)S(1)}, bf16[16,7168]{1,0:T(8,128)(2,1)}, u32[]{:S(2)}) copy-start(bf16[16,7168]{1,0:T(8,128)(2,1)} %param.8) | copy-start | bytes 688132
  16.9 59.4 %all-to-all-start = ((bf16[128,5,1792]{2,1,0:T(8,128)(2,1)}), bf16[128,5,1792]{2,1,0:T(8,128)(2,1)}, u32[]{:S(2)}, u32[]{:S(2)}) async-start(bf16[128,5,1792]{2,1,0:T(8,128)(2,1)} %bitcast.51), calls=%async_computation | async-start | bytes 7340032 | tf_op jit(solution)/shard_map/all_to_all | solution.py:59
  76.4 52.3 %all-to-all-start.1 = ((bf16[128,5,1792]{2,1,0:T(8,128)(2,1)}), bf16[128,5,1792]{2,1,0:T(8,128)(2,1)}, u32[]{:S(2)}, u32[]{:S(2)}) async-start(bf16[128,5,1792]{2,1,0:T(8,128)(2,1)} %bitcast.50), calls=%async_computation.1 | async-start | bytes 7340032 | tf_op jit(solution)/shard_map/all_to_all | solution.py:60
  81.1 333.3 %all-gather.3.cloned.1.call-start = ((), (), s32[]{:S(2)}) async-start(), calls=%async_computation.3 | async-start | bytes 39321600 | tf_op jit(solution)/shard_map/all_gather | solution.py:9
  86.7 5.4 %copy-start.3 = (bf16[640,1792]{1,0:T(8,128)(2,1)S(1)}, bf16[640,1792]{1,0:T(8,128)(2,1)}, u32[]{:S(2)}) copy-start(bf16[640,1792]{1,0:T(8,128)(2,1)} %reshape.47) | copy-start | bytes 6881284
  86.7 5.4 %copy-start.12 = (bf16[1,1792,1024]{2,1,0:T(8,128)(2,1)S(1)}, bf16[1,1792,1024]{2,1,0:T(8,128)(2,1)}, u32[]{:S(2)}) copy-start(bf16[1,1792,1024]{2,1,0:T(8,128)(2,1)} %param.11) | copy-start | bytes 11010052
  134.0 5.4 %copy-start.2 = (f32[640,1024]{1,0:T(8,128)S(1)}, f32[640,1024]{1,0:T(8,128)}, u32[]{:S(2)}) copy-start(f32[640,1024]{1,0:T(8,128)} %fusion.9) | copy-start | bytes 7864324
  429.5 5.1 copy-start.11
  434.6 2.6 copy-start.6
  434.6 2.6 copy-start.8
  434.6 3.0 copy-start.13
  443.1 9.8 %copy-start.4 = (bf16[640,1792]{1,0:T(8,128)(2,1)S(1)}, bf16[640,1792]{1,0:T(8,128)(2,1)}, u32[]{:S(2)}) copy-start(bf16[640,1792]{1,0:T(8,128)(2,1)} %reshape.47) | copy-start | bytes 6881284
  443.1 57.4 %all-to-all-start.2 = ((bf16[128,5,1792]{2,1,0:T(8,128)(2,1)}), bf16[128,5,1792]{2,1,0:T(8,128)(2,1)}, u32[]{:S(2)}, u32[]{:S(2)}) async-start(bf16[128,5,1792]{2,1,0:T(8,128)(2,1)} %reshape.51), calls=%async_computation.2 | async-start | bytes 7340032 | tf_op jit(solution)/shard_map/all_to_all | solution.py:90
  452.9 6.0 %copy-start.7 = (bf16[640,1024]{1,0:T(8,128)(2,1)S(1)}, bf16[640,1024]{1,0:T(8,128)(2,1)}, u32[]{:S(2)}) copy-start(bf16[640,1024]{1,0:T(8,128)(2,1)} %copy-done.6) | copy-start | bytes 3932164
  458.9 4.5 copy-start.5
  503.4 1.4 copy-start.1
Sparse Core Ops, SparseCore 0:
  143.0 271.3 all-gather.2
